TPU v7x, 512 devices: a whole 4x8x8 slice. The times are simulated.
512 devices in a mesh: pool: 64 (over x, z, core), mp: 8 (over y).
Axes of the slice: x: 4, y: 8, z: 8, core: 2. Of those that a mesh axis runs over, the one named last changes fastest.
Arguments:
- residual_in: bfloat16 [16384, 2048], P('pool', 'mp'), may hold values from -6 to 6
- mlp_branch: bfloat16 [16384, 2048], P('pool'), may hold values from -6 to 6
- norm_gain: float32 [2048], replicated, may hold values from 0.5 to 1.5
- norm_bias: float32 [2048], replicated, may hold values from -3 to 3
- w_qkv: bfloat16 [2048, 3, 2048], P('pool', None, 'mp'), may hold values from -0.125 to 0.125
- qkv_bias: float32 [3, 2048], P(None, 'mp'), may hold values from -3 to 3
- cache_pool: bfloat16 [3072, 2, 32, 2048], P('pool', None, None, 'mp'), as said below
- w_dense: bfloat16 [2048, 2048], P('mp', 'pool'), may hold values from -0.125 to 0.125
- dense_bias: float32 [2048], replicated, may hold values from -3 to 3
- next_gain: float32 [2048], replicated, may hold values from 0.5 to 1.5
- next_bias: float32 [2048], replicated, may hold values from -3 to 3
- w_next: bfloat16 [2048, 3, 2048], P('pool', None, 'mp'), may hold values from -0.125 to 0.125
- next_qkv_bias: float32 [3, 2048], P(None, 'mp'), may hold values from -3 to 3
- token_request: int32 [16384], P('pool'), may hold values from 0 to 255, as said below
- cache_len: int32 [256], P('pool'), may hold values from 0 to 1024, as said below
- block_table: int32 [256, 32], P('pool'), may hold values from 0 to 3071, as said below
Outputs:
- hidden_out: bfloat16 [16384, 2048], P('pool', 'mp')
- next_qkv: bfloat16 [16384, 3, 2048], P('pool', None, 'mp')
Inputs may be any that keep to these rules, and one draw needn't show every extreme that they name: `token_request`: the 256 tokens of index i of pool belong to the requests i * 4 to (i+1) * 4 - 1, each request's tokens in one run, in increasing order, each request with at least one token. `cache_len`: 0 for a fresh prompt; some request has exactly 1024. `block_table`: block b is held by index b // 48 of pool; a block may appear in several lists; entries at or past a request's cached blocks are padding. Of the 128 entries of the requests of one index of pool, exactly 2 name blocks held by each index of pool. `cache_pool`: cached keys and values.
All inputs are finite; a program needn't handle non-finite values.
Results may differ from a plain program's by a relative error of at most 0.015.
Values may be sent and summed in bfloat16 or wider, within the bound.
No kernel may reach another device: no remote copies, remote signals or barrier semaphores. Data moves between devices by JAX's collectives and lax.ppermute only.
A program may use at most 128 MiB of HBM per device.

v0:
```python
import jax
import jax.numpy as jnp
from jax import lax
from jax.sharding import PartitionSpec as P

HEAD_DIM = 64
ROT = 32
epsilon = 1e-05


def layer_norm(row_data, gain_vec, bias_vec):
    values = row_data.astype(jnp.float32)
    row_mean = jnp.mean(values, axis=-1, keepdims=True)
    centered = values - row_mean
    spread = jnp.mean(centered * centered, axis=-1, keepdims=True)
    return centered * lax.rsqrt(spread + epsilon) * gain_vec + bias_vec


def rotate(head_rows, positions):
    half_rot = ROT // 2
    inverse = 10000.0 ** (-2.0 * jnp.arange(half_rot, dtype=jnp.float32) / ROT)
    angles = positions.astype(jnp.float32)[:, None] * inverse[None, :]
    cosine = jnp.cos(angles)[:, None, :]
    sine = jnp.sin(angles)[:, None, :]
    lower = head_rows[..., :half_rot]
    upper = head_rows[..., half_rot:ROT]
    return jnp.concatenate(
        [lower * cosine - upper * sine, upper * cosine + lower * sine, head_rows[..., ROT:]],
        axis=-1,
    )


def run_starts(token_request):
    tok_total = token_request.shape[0]
    token_index = jnp.arange(tok_total, dtype=jnp.int32)
    change = jnp.concatenate([jnp.ones((1,), dtype=bool), token_request[1:] != token_request[:-1]])
    return (token_index, lax.cummax(jnp.where(change, token_index, 0), axis=0))


def row_folder(left_rows, running, w_piece):
    columns_part = lax.slice_in_dim(left_rows, 0, w_piece.shape[0], axis=1)
    return running + jnp.dot(
        columns_part, w_piece.reshape(w_piece.shape[0], -1), preferred_element_type=jnp.float32
    )


def local(
    residual_in,
    mlp_branch,
    norm_gain,
    norm_bias,
    w_qkv,
    qkv_bias,
    cache_pool,
    w_dense,
    dense_bias,
    next_gain,
    next_bias,
    w_next,
    next_qkv_bias,
    token_request,
    cache_len,
    block_table,
):
    full_rows = lax.all_gather(residual_in, "mp", axis=1, tiled=True)
    tok_count = full_rows.shape[0]
    col_width = w_qkv.shape[2]
    head_count = col_width // HEAD_DIM
    normed = layer_norm(full_rows, norm_gain, norm_bias).astype(jnp.bfloat16)
    empty_sum = jnp.zeros((tok_count, 3 * col_width), jnp.float32)
    projected = row_folder(normed, empty_sum, lax.all_gather(w_qkv, "pool", axis=0, tiled=True))
    projected = (projected + qkv_bias.reshape(1, 3 * col_width)).reshape(tok_count, 3, col_width)
    token_index, starts = run_starts(token_request)
    request_count = cache_len.shape[0]
    local_req = token_request - request_count * lax.axis_index("pool")
    request_ids = jnp.arange(request_count, dtype=jnp.int32)
    request_match = local_req[:, None] == request_ids[None, :]
    cached_here = jnp.sum(jnp.where(request_match, cache_len[None, :], 0), axis=1)
    positions = cached_here + token_index - starts
    query = rotate(projected[:, 0].reshape(tok_count, head_count, HEAD_DIM), positions).astype(
        jnp.bfloat16
    )
    key_new = rotate(projected[:, 1].reshape(tok_count, head_count, HEAD_DIM), positions).astype(
        jnp.bfloat16
    )
    value_new = projected[:, 2].reshape(tok_count, head_count, HEAD_DIM).astype(jnp.bfloat16)
    pool_count = lax.axis_size("pool")
    blocks_here = cache_pool.shape[0]
    entries = block_table.reshape(-1)
    holder_order = jnp.argsort(entries // blocks_here, stable=True)
    slot_ids = (entries % blocks_here)[holder_order].reshape(pool_count, -1)
    wanted = lax.all_to_all(slot_ids, "pool", split_axis=0, concat_axis=0, tiled=True)
    packed = cache_pool[wanted.reshape(-1)].reshape((pool_count, -1) + cache_pool.shape[1:])
    arrived = lax.all_to_all(packed, "pool", split_axis=0, concat_axis=0, tiled=True)
    table_blocks = arrived.reshape((-1,) + cache_pool.shape[1:])[jnp.argsort(holder_order)]
    span = block_table.shape[1] * cache_pool.shape[2]
    slot_total = request_count * span
    cached_keys = table_blocks[:, 0].reshape(slot_total, head_count, HEAD_DIM)
    cached_values = table_blocks[:, 1].reshape(slot_total, head_count, HEAD_DIM)
    slot_index = jnp.arange(slot_total, dtype=jnp.int32)
    slot_req = slot_index // span
    slot_len = jnp.repeat(cache_len, span, total_repeat_length=slot_total)
    cache_ok = (slot_req[None, :] == local_req[:, None]) & (slot_index % span < slot_len)[None, :]
    new_ok = (token_request[None, :] == token_request[:, None]) & (
        token_index[None, :] <= token_index[:, None]
    )
    allowed = jnp.concatenate([cache_ok, new_ok], axis=1)
    key_all = jnp.concatenate([cached_keys, key_new], axis=0).transpose(1, 0, 2)
    value_all = jnp.concatenate([cached_values, value_new], axis=0).transpose(1, 0, 2)
    score_scale = HEAD_DIM ** (-0.5)

    def one_head(operands):
        q_head, k_head, v_head = operands
        scores = (
            jnp.einsum("qd,kd->qk", q_head, k_head, preferred_element_type=jnp.float32)
            * score_scale
        )
        scores = jnp.where(allowed, scores, -1e30)
        row_max = jnp.max(scores, axis=1, keepdims=True)
        weights = jnp.exp(scores - row_max)
        probs = (weights / jnp.sum(weights, axis=1, keepdims=True)).astype(jnp.bfloat16)
        return jnp.dot(probs, v_head, preferred_element_type=jnp.float32).astype(jnp.bfloat16)

    mixed = lax.map(one_head, (query.transpose(1, 0, 2), key_all, value_all))
    attended = mixed.transpose(1, 0, 2).reshape(tok_count, col_width)
    partial_out = jnp.dot(
        attended,
        lax.all_gather(w_dense, "pool", axis=1, tiled=True),
        preferred_element_type=jnp.float32,
    )
    mp_index = lax.axis_index("mp")
    dense_total = lax.psum(partial_out.astype(jnp.bfloat16), "mp").astype(jnp.float32)
    whole_hidden = (
        full_rows.astype(jnp.float32) + dense_total + dense_bias + mlp_branch.astype(jnp.float32)
    ).astype(jnp.bfloat16)
    hidden_out = lax.dynamic_slice_in_dim(whole_hidden, mp_index * col_width, col_width, 1)
    normed_next = layer_norm(whole_hidden, next_gain, next_bias).astype(jnp.bfloat16)
    next_raw = row_folder(
        normed_next, empty_sum, lax.all_gather(w_next, "pool", axis=0, tiled=True)
    )
    next_qkv = (
        (next_raw + next_qkv_bias.reshape(1, 3 * col_width))
        .astype(jnp.bfloat16)
        .reshape(tok_count, 3, col_width)
    )
    return (hidden_out, next_qkv)


def solution(mesh):
    in_specs = (
        P("pool", "mp"),
        P("pool", None),
        P(),
        P(),
        P("pool", None, "mp"),
        P(None, "mp"),
        P("pool", None, None, "mp"),
        P("mp", "pool"),
        P(),
        P(),
        P(),
        P("pool", None, "mp"),
        P(None, "mp"),
        P("pool"),
        P("pool"),
        P("pool", None),
    )
    out_specs = (P("pool", "mp"), P("pool", None, "mp"))
    return jax.shard_map(local, mesh=mesh, in_specs=in_specs, out_specs=out_specs, check_vma=False)
```

profile of v0, /device:TPU:2, one launch (start us, length us, event | category | flops | bytes accessed | tf_op | source)
XLA Modules:
  0.0 420.4 jit_solution(15002149205869213757)
XLA Ops:
  7.2 0.7 all-gather.5.cloned.1.call-update
  8.0 0.7 all-gather.7.cloned.1.call-update
  8.7 0.7 broadcast_divide_fusion
  9.5 0.7 sign_compare_fusion
  10.3 2.5 sort.34
  12.9 1.2 gather_fusion
  14.2 22.3 %all_to_all.14 = s32[64,1,2]{2,1,0:T(1,128)S(1)} all-to-all(s32[64,1,2]{2,1,0:T(1,128)S(1)} %bitcast.83), channel_id=1, replica_groups=mesh['pool'=64,'mp'=8] {'pool'}, dimensions={0} | all-to-all | bytes 1024 | tf_op jit(solution)/shard_map/all_to_all | solution.py:92
  37.0 0.7 reduce.7
  37.9 2.8 gather_fusion.1
  40.7 6.6 %all-to-all-start.1 = ((bf16[64,2,2,32,256]{4,3,2,1,0:T(8,128)(2,1)}), bf16[64,2,2,32,256]{4,3,2,1,0:T(8,128)(2,1)}, u32[]{:S(2)}, u32[]{:S(2)}) async-start(bf16[64,2,2,32,256]{4,3,2,1,0:T(8,128)(2,1)} %bitcast.71), calls=%async_computation.1 | async-start | bytes 8388608 | tf_op jit(solution)/shard_map/all_to_all | solution.py:94
  49.6 2.5 sort.35
  53.1 2.5 fusion.51
  55.8 0.8 compare_and_fusion
  56.8 1.4 convert_reduce_fusion
  58.2 1.6 fusion.22
  59.9 97.4 %all-gather.7.cloned.1.call-done = bf16[2048,3,256]{2,0,1:T(8,128)(2,1)} async-done(((bf16[32,3,256]{2,0,1:T(8,128)(2,1)}), bf16[2048,3,256]{2,0,1:T(8,128)(2,1)}) %all-gather.7.cloned.1.call-update) | async-done | bytes 3145744 | tf_op jit(solution)/shard_map/all_gather | solution.py:71
  157.3 4.7 %copy.69 = bf16[2048,3,256]{0,2,1:T(8,128)(2,1)} copy(bf16[2048,3,256]{2,0,1:T(8,128)(2,1)} %all-gather.7.cloned.1.call-done) | data formatting | bytes 6291456 | tf_op jit(solution)/shard_map/all_gather | solution.py:71
  162.1 4.0 convolution_add_fusion.1
  166.0 1.4 copy.70
  168.0 5.0 %gather_fusion.2 = bf16[128,2,32,256]{3,2,1,0:T(8,128)(2,1)} fusion(bf16[128,2,32,256]{3,2,1,0:T(8,128)(2,1)} %bitcast.13, s32[1024]{0:T(1024)S(1)} %pad_clamp_fusion), kind=kCustom, calls=%fused_computation.2 | custom fusion | bytes 8389120 | tf_op jit(solution)/shard_map/gather | solution.py:95
  173.0 4.7 %fusion.58 = (bf16[128,1,32,256]{3,2,1,0:T(8,128)(2,1)}, bf16[128,1,32,256]{3,2,1,0:T(8,128)(2,1)}) fusion(bf16[128,2,32,256]{3,2,1,0:T(8,128)(2,1)} %gather_fusion.2), kind=kLoop, calls=%fused_computation.109 | loop fusion | bytes 8388608 | tf_op jit(solution)/shard_map/slice | solution.py:99
  177.6 7.1 %reshape_squeeze.14 = bf16[4096,4,64]{2,1,0:T(4,128)(2,1)} reshape(bf16[128,1,32,256]{3,2,1,0:T(8,128)(2,1)} %get-tuple-element.110) | data formatting | bytes 4194304 | tf_op jit(solution)/shard_map/reshape;squeeze | solution.py:98
  184.7 17.6 %maximum_bitcast_fusion = bf16[4,4352,64]{2,0,1:T(4,128)(2,1)S(1)} fusion(bf16[256,4,64]{2,1,0:T(4,128)(2,1)S(1)} %copy.72, bf16[4096,4,64]{2,1,0:T(4,128)(2,1)} %reshape_squeeze.14), kind=kLoop, calls=%fused_computation.20 | loop fusion | flops 1114112 | bytes 4456448 | tf_op jit(solution)/shard_map/transpose | solution.py:108
  202.4 2.7 copy.75
  205.1 7.1 %reshape_squeeze.16 = bf16[4096,4,64]{2,1,0:T(4,128)(2,1)} reshape(bf16[128,1,32,256]{3,2,1,0:T(8,128)(2,1)} %get-tuple-element.109) | data formatting | bytes 4194304 | tf_op jit(solution)/shard_map/reshape;squeeze | solution.py:99
  212.1 17.6 %maximum_bitcast_fusion.1 = bf16[4,4352,64]{2,0,1:T(4,128)(2,1)S(1)} fusion(bf16[256,4,64]{2,1,0:T(4,128)(2,1)S(1)} %copy.73, bf16[4096,4,64]{2,1,0:T(4,128)(2,1)} %reshape_squeeze.16), kind=kLoop, calls=%fused_computation.21 | loop fusion | flops 1114112 | bytes 4456448 | tf_op jit(solution)/shard_map/transpose | solution.py:109
  229.8 2.7 copy.76
  232.5 21.9 %while.11 = (s32[]{:T(128)}, bf16[4,256,64]{1,2,0:T(8,128)(2,1)S(1)}, bf16[4,256,64]{1,2,0:T(8,128)(2,1)S(1)}, bf16[4,4352,64]{2,1,0:T(8,128)(2,1)}, pred[256,43...) while((s32[]{:T(128)}, bf16[4,256,64]{1,2,0:T(8,128)(2,1)S(1)}, ...), condition=%wide.region_10.11_spmd, body=%wide.region_7.10_spmd.sunk | while | flops 294141440 | bytes 16784460 | solution.py:124
  232.5 2.4 fusion.70
  234.8 0.8 fusion.71
  235.6 2.4 fusion.72
  238.0 2.3 fusion.70
  240.3 0.8 fusion.71
  241.1 2.4 fusion.72
  243.4 2.3 fusion.70
  245.8 0.8 fusion.71
  246.5 2.4 fusion.72
  248.9 2.3 fusion.70
  251.3 0.8 fusion.71
  252.0 2.4 fusion.72
  254.4 2.7 convolution_convert_fusion
  257.2 68.4 %all-gather.11.cloned.1.call-done = bf16[2048,3,256]{2,0,1:T(8,128)(2,1)} async-done(((bf16[32,3,256]{2,0,1:T(8,128)(2,1)}), bf16[2048,3,256]{2,0,1:T(8,128)(2,1)}) %all-gather.11.cloned.1.call-update) | async-done | bytes 3145744 | tf_op jit(solution)/shard_map/all_gather | solution.py:139
  325.6 4.7 %copy.77 = bf16[2048,3,256]{0,2,1:T(8,128)(2,1)} copy(bf16[2048,3,256]{2,0,1:T(8,128)(2,1)} %all-gather.11.cloned.1.call-done) | data formatting | bytes 6291456 | tf_op jit(solution)/shard_map/all_gather | solution.py:139
  330.3 76.7 %all-reduce.2.cloned.1.call-done = bf16[256,2048]{1,0:T(8,128)(2,1)} async-done(((bf16[256,2048]{1,0:T(8,128)(2,1)}), bf16[256,2048]{1,0:T(8,128)(2,1)}) %all-reduce.2.cloned.1.call-update) | async-done | bytes 1048592 | tf_op jit(solution)/shard_map/psum | solution.py:132
  407.0 2.0 convert_reduce_fusion.1
  410.1 1.2 fusion.33
  411.4 0.9 copy.79
  412.3 1.6 constant_dynamic-slice_fusion
  (96 shorter events, 6.4 us)
Async XLA Ops:
  7.2 30.8 %copy-start = (bf16[48,2,32,256]{3,2,1,0:T(8,128)(2,1)S(1)}, bf16[48,2,32,256]{3,2,1,0:T(8,128)(2,1)}, u32[]{:S(2)}) copy-start(bf16[48,2,32,256]{3,2,1,0:T(8,128)(2,1)} %param.26) | copy-start | bytes 4718596
  7.2 49.6 %all-gather.5.cloned.1.call-start = ((), (), s32[]{:S(2)}) async-start(), calls=%async_computation.2 | async-start | bytes 1179648 | tf_op jit(solution)/shard_map/all_gather | solution.py:65
  7.9 149.4 %all-gather.7.cloned.1.call-start = ((), (), s32[]{:S(2)}) async-start(), calls=%async_computation.3 | async-start | bytes 3194880 | tf_op jit(solution)/shard_map/all_gather | solution.py:71
  40.7 8.2 %copy-start.10 = (f32[3,256]{1,0:T(4,128)S(1)}, f32[3,256]{1,0:T(4,128)}, u32[]{:S(2)}) copy-start(f32[3,256]{1,0:T(4,128)} %param.25) | copy-start | bytes 9220
  40.7 8.3 %copy-start.7 = (s32[256]{0:T(256)S(1)}, s32[256]{0:T(256)}, u32[]{:S(2)}) copy-start(s32[256]{0:T(256)} %param.33) | copy-start | bytes 3076
  40.7 11.5 %copy-start.8 = (s32[4]{0:T(128)S(1)}, s32[4]{0:T(128)}, u32[]{:S(2)}) copy-start(s32[4]{0:T(128)} %param.34) | copy-start | bytes 52
  40.7 12.3 %copy-start.12 = (pred[4096]{0:T(1024)(128)(4,1)S(1)}, pred[4096]{0:T(1024)(128)(4,1)}, u32[]{:S(2)}) copy-start(pred[4096]{0:T(1024)(128)(4,1)} %constant.223) | copy-start | bytes 12292
  40.7 12.3 %copy-start.13 = (pred[4096]{0:T(1024)(128)(4,1)S(1)}, pred[4096]{0:T(1024)(128)(4,1)}, u32[]{:S(2)}) copy-start(pred[4096]{0:T(1024)(128)(4,1)} %constant.224) | copy-start | bytes 12292
  40.7 12.3 %copy-start.14 = (pred[4096]{0:T(1024)(128)(4,1)S(1)}, pred[4096]{0:T(1024)(128)(4,1)}, u32[]{:S(2)}) copy-start(pred[4096]{0:T(1024)(128)(4,1)} %constant.225) | copy-start | bytes 12292
  40.7 127.2 %all-to-all-start.1 = ((bf16[64,2,2,32,256]{4,3,2,1,0:T(8,128)(2,1)}), bf16[64,2,2,32,256]{4,3,2,1,0:T(8,128)(2,1)}, u32[]{:S(2)}, u32[]{:S(2)}) async-start(bf16[64,2,2,32,256]{4,3,2,1,0:T(8,128)(2,1)} %bitcast.71), calls=%async_computation.1 | async-start | bytes 8388608 | tf_op jit(solution)/shard_map/all_to_all | solution.py:94
  47.4 207.0 %all-gather.9.cloned.1.call-start = ((), (), s32[]{:S(2)}) async-start(), calls=%async_computation.4 | async-start | bytes 1064960 | tf_op jit(solution)/shard_map/all_gather | solution.py:128
  48.1 277.5 %all-gather.11.cloned.1.call-start = ((), (), s32[]{:S(2)}) async-start(), calls=%async_computation.6 | async-start | bytes 3194880 | tf_op jit(solution)/shard_map/all_gather | solution.py:139
  48.7 358.3 %all-reduce.2.cloned.1.call-start = ((), (), s32[]{:S(2)}) async-start(), calls=%async_computation.5 | async-start | bytes 2097152 | tf_op jit(solution)/shard_map/psum | solution.py:132
  59.9 102.2 %copy-start.2 = (bf16[256,2048]{1,0:T(8,128)(2,1)S(1)}, bf16[256,2048]{1,0:T(8,128)(2,1)}, u32[]{:S(2)}) copy-start(bf16[256,2048]{1,0:T(8,128)(2,1)} %all-gather.5.cloned.1.call-done) | copy-start | bytes 3145732
  59.9 102.2 %copy-start.15 = (f32[2048]{0:T(1024)S(1)}, f32[2048]{0:T(1024)}, u32[]{:S(2)}) copy-start(f32[2048]{0:T(1024)} %param.23) | copy-start | bytes 24580
  59.9 102.2 %copy-start.16 = (f32[2048]{0:T(1024)S(1)}, f32[2048]{0:T(1024)}, u32[]{:S(2)}) copy-start(f32[2048]{0:T(1024)} %param.22) | copy-start | bytes 24580
  229.8 2.7 copy-start.6
  254.4 2.8 copy-start.11
  257.2 149.8 %copy-start.5 = (bf16[256,2048]{1,0:T(8,128)(2,1)S(1)}, bf16[256,2048]{1,0:T(8,128)(2,1)}, u32[]{:S(2)}) copy-start(bf16[256,2048]{1,0:T(8,128)(2,1)} %param.21) | copy-start | bytes 3145732
  257.2 149.8 %copy-start.9 = (f32[2048]{0:T(1024)S(1)}, f32[2048]{0:T(1024)}, u32[]{:S(2)}) copy-start(f32[2048]{0:T(1024)} %param.28) | copy-start | bytes 24580
  330.3 79.8 %copy-start.17 = (f32[2048]{0:T(1024)S(1)}, f32[2048]{0:T(1024)}, u32[]{:S(2)}) copy-start(f32[2048]{0:T(1024)} %param.30) | copy-start | bytes 24580
  330.3 79.8 %copy-start.18 = (f32[2048]{0:T(1024)S(1)}, f32[2048]{0:T(1024)}, u32[]{:S(2)}) copy-start(f32[2048]{0:T(1024)} %param.29) | copy-start | bytes 24580
  407.0 3.0 copy-start.4
  409.1 1.0 copy-start.3
  409.5 4.4 %copy-start.1 = (bf16[48,2,32,256]{3,2,1,0:T(8,128)(2,1)S(1)}, bf16[48,2,32,256]{3,2,1,0:T(8,128)(2,1)}, u32[]{:S(2)}) copy-start(bf16[48,2,32,256]{3,2,1,0:T(8,128)(2,1)} %param.26) | copy-start | bytes 4718596
Sparse Core Ops, SparseCore 0:
  10.0 46.6 all-gather.4
  60.1 97.1 all-gather.6
  160.7 80.2 all-gather.8
  244.2 81.3 all-gather.10
  327.8 79.2 all-reduce.1
where the time goes:
time: 422 us; the launch traced here: 420 us
  waiting for transfers between devices  245 us (58%)
  other arithmetic  55.4 us (13%)
  local copies, waits for them, and re-layouts  49.6 us (12%)
  matrix products  26.7 us (6%)
  blocking collectives  22.3 us (5%)
  between operations  14.2 us (3%)
  starting transfers between devices  7.01 us (2%)
    all_gather x1, waiting for transfers between devices, local(): lax.all_gather(w_qkv, 'pool', axis=0, tiled=True)  97.4 us
    psum x1, waiting for transfers between devices, local(): lax.psum(partial_out.astype(jnp.bfloat16), 'mp').astype(jnp.float32)  76.7 us
    all_gather x1, waiting for transfers between devices, local(): lax.all_gather(w_next, 'pool', axis=0, tiled=True)  68.4 us
    all_to_all x1, blocking collectives, local(): lax.all_to_all(slot_ids, 'pool', split_axis=0, concat_axis=0, tiled=True)  22.3 us
    transpose x1, other arithmetic, local(): jnp.concatenate([cached_values, value_new], axis=0).transpose(1, 0, 2)  17.6 us
    transpose x1, other arithmetic, local(): key_all = jnp.concatenate([cached_keys, key_new], axis=0).transpose(1, 0, 2)  17.6 us
    dot_general x4, matrix products, one_head(): jnp.dot(probs, v_head, preferred_element_type=jnp.float32)  9.42 us
    dot_general x4, matrix products, one_head(): jnp.einsum('qd,kd->qk', q_head, k_head, preferred_element_type=jnp.float32)  9.39 us
  transfers between devices with their start and end apart: 6, of which 4 were waited for; matrix products, arithmetic and copies ran while one was open for 30% of the time, Pallas kernels for 0%

commit v1 on v0

--- a/solution.py
+++ b/solution.py
@@ -129,7 +129,8 @@
         preferred_element_type=jnp.float32,
     )
     mp_index = lax.axis_index("mp")
-    dense_total = lax.psum(partial_out.astype(jnp.bfloat16), "mp").astype(jnp.float32)
+    feed_arrays_up = lambda sheet, peer_axis: jnp.sum(lax.all_gather(sheet, peer_axis), 0)
+    dense_total = feed_arrays_up(partial_out.astype(jnp.bfloat16), "mp").astype(jnp.float32)
     whole_hidden = (
         full_rows.astype(jnp.float32) + dense_total + dense_bias + mlp_branch.astype(jnp.float32)
     ).astype(jnp.bfloat16)

time: 422 us -> 443 us (1.050)
  the two profiles are of different devices: /device:TPU:2 before, /device:TPU:1 now
where the time goes in v1:
time: 443 us; the launch traced here: 442 us
  waiting for transfers between devices  260 us (59%)
  other arithmetic  60.6 us (14%)
  local copies, waits for them, and re-layouts  49.5 us (11%)
  matrix products  26.7 us (6%)
  blocking collectives  23.9 us (5%)
  between operations  14.2 us (3%)
  starting transfers between devices  6.2 us (1%)
    all_gather x1, waiting for transfers between devices, local(): lax.all_gather(w_qkv, 'pool', axis=0, tiled=True)  98.1 us
    all_gather x1, waiting for transfers between devices, local(): lax.all_gather(sheet, peer_axis)  90.1 us
    all_gather x1, waiting for transfers between devices, local(): lax.all_gather(w_next, 'pool', axis=0, tiled=True)  69.4 us
    all_to_all x1, blocking collectives, local(): lax.all_to_all(slot_ids, 'pool', split_axis=0, concat_axis=0, tiled=True)  23.9 us
    transpose x1, other arithmetic, local(): key_all = jnp.concatenate([cached_keys, key_new], axis=0).transpose(1, 0, 2)  17.6 us
    transpose x1, other arithmetic, local(): jnp.concatenate([cached_values, value_new], axis=0).transpose(1, 0, 2)  17.6 us
    dot_general x4, matrix products, one_head(): jnp.dot(probs, v_head, preferred_element_type=jnp.float32)  9.41 us
    dot_general x4, matrix products, one_head(): jnp.einsum('qd,kd->qk', q_head, k_head, preferred_element_type=jnp.float32)  9.38 us
  transfers between devices with their start and end apart: 6, of which 3 were waited for; matrix products, arithmetic and copies ran while one was open for 28% of the time, Pallas kernels for 0%

profile of v1, /device:TPU:1, one launch (start us, length us, event | category | flops | bytes accessed | tf_op | source)
XLA Modules:
  0.0 441.5 jit_solution(10922649553515001867)
XLA Ops:
  8.0 0.7 all-gather.9.cloned.1.call-update
  8.7 0.7 broadcast_divide_fusion
  9.5 0.7 sign_compare_fusion
  10.3 2.5 sort.34
  12.9 1.2 gather_fusion
  14.2 23.9 %all_to_all.14 = s32[64,1,2]{2,1,0:T(1,128)S(1)} all-to-all(s32[64,1,2]{2,1,0:T(1,128)S(1)} %bitcast.85), channel_id=1, replica_groups=mesh['pool'=64,'mp'=8] {'pool'}, dimensions={0} | all-to-all | bytes 1024 | tf_op jit(solution)/shard_map/all_to_all | solution.py:92
  38.7 0.7 reduce.8
  39.6 2.8 gather_fusion.1
  42.4 5.8 %all-to-all-start.1 = ((bf16[64,2,2,32,256]{4,3,2,1,0:T(8,128)(2,1)}), bf16[64,2,2,32,256]{4,3,2,1,0:T(8,128)(2,1)}, u32[]{:S(2)}, u32[]{:S(2)}) async-start(bf16[64,2,2,32,256]{4,3,2,1,0:T(8,128)(2,1)} %bitcast.72), calls=%async_computation.1 | async-start | bytes 8388608 | tf_op jit(solution)/shard_map/all_to_all | solution.py:94
  50.4 2.5 sort.35
  53.9 2.5 fusion.51
  56.7 0.7 compare_and_fusion
  57.6 1.4 convert_reduce_fusion
  59.0 1.6 fusion.22
  60.7 98.1 %all-gather.9.cloned.1.call-done = bf16[2048,3,256]{2,0,1:T(8,128)(2,1)} async-done(((bf16[32,3,256]{2,0,1:T(8,128)(2,1)}), bf16[2048,3,256]{2,0,1:T(8,128)(2,1)}) %all-gather.9.cloned.1.call-update) | async-done | bytes 3145744 | tf_op jit(solution)/shard_map/all_gather | solution.py:71
  158.8 4.7 %copy.69 = bf16[2048,3,256]{0,2,1:T(8,128)(2,1)} copy(bf16[2048,3,256]{2,0,1:T(8,128)(2,1)} %all-gather.9.cloned.1.call-done) | data formatting | bytes 6291456 | tf_op jit(solution)/shard_map/all_gather | solution.py:71
  163.5 4.0 convolution_add_fusion.1
  167.5 1.4 copy.70
  169.5 5.0 %gather_fusion.2 = bf16[128,2,32,256]{3,2,1,0:T(8,128)(2,1)} fusion(bf16[128,2,32,256]{3,2,1,0:T(8,128)(2,1)} %bitcast.13, s32[1024]{0:T(1024)S(1)} %pad_clamp_fusion), kind=kCustom, calls=%fused_computation.2 | custom fusion | bytes 8389120 | tf_op jit(solution)/shard_map/gather | solution.py:95
  174.4 4.7 %fusion.58 = (bf16[128,1,32,256]{3,2,1,0:T(8,128)(2,1)}, bf16[128,1,32,256]{3,2,1,0:T(8,128)(2,1)}) fusion(bf16[128,2,32,256]{3,2,1,0:T(8,128)(2,1)} %gather_fusion.2), kind=kLoop, calls=%fused_computation.109 | loop fusion | bytes 8388608 | tf_op jit(solution)/shard_map/slice | solution.py:99
  179.1 7.1 %reshape_squeeze.14 = bf16[4096,4,64]{2,1,0:T(4,128)(2,1)} reshape(bf16[128,1,32,256]{3,2,1,0:T(8,128)(2,1)} %get-tuple-element.110) | data formatting | bytes 4194304 | tf_op jit(solution)/shard_map/reshape;squeeze | solution.py:98
  186.2 17.6 %maximum_bitcast_fusion = bf16[4,4352,64]{2,0,1:T(4,128)(2,1)S(1)} fusion(bf16[256,4,64]{2,1,0:T(4,128)(2,1)S(1)} %copy.72, bf16[4096,4,64]{2,1,0:T(4,128)(2,1)} %reshape_squeeze.14), kind=kLoop, calls=%fused_computation.20 | loop fusion | flops 1114112 | bytes 4456448 | tf_op jit(solution)/shard_map/transpose | solution.py:108
  203.9 2.7 copy.75
  206.5 7.1 %reshape_squeeze.16 = bf16[4096,4,64]{2,1,0:T(4,128)(2,1)} reshape(bf16[128,1,32,256]{3,2,1,0:T(8,128)(2,1)} %get-tuple-element.109) | data formatting | bytes 4194304 | tf_op jit(solution)/shard_map/reshape;squeeze | solution.py:99
  213.6 17.6 %maximum_bitcast_fusion.1 = bf16[4,4352,64]{2,0,1:T(4,128)(2,1)S(1)} fusion(bf16[256,4,64]{2,1,0:T(4,128)(2,1)S(1)} %copy.73, bf16[4096,4,64]{2,1,0:T(4,128)(2,1)} %reshape_squeeze.16), kind=kLoop, calls=%fused_computation.21 | loop fusion | flops 1114112 | bytes 4456448 | tf_op jit(solution)/shard_map/transpose | solution.py:109
  231.3 2.7 copy.76
  234.0 21.9 %while.11 = (s32[]{:T(128)}, bf16[4,256,64]{1,2,0:T(8,128)(2,1)S(1)}, bf16[4,256,64]{1,2,0:T(8,128)(2,1)S(1)}, bf16[4,4352,64]{2,1,0:T(8,128)(2,1)}, pred[256,43...) while((s32[]{:T(128)}, bf16[4,256,64]{1,2,0:T(8,128)(2,1)S(1)}, ...), condition=%wide.region_10.11_spmd, body=%wide.region_7.10_spmd.sunk | while | flops 294141440 | bytes 16784460 | solution.py:124
  234.0 2.3 fusion.70
  236.3 0.8 fusion.71
  237.1 2.4 fusion.72
  239.4 2.3 fusion.70
  241.8 0.8 fusion.71
  242.5 2.3 fusion.72
  244.9 2.3 fusion.70
  247.3 0.8 fusion.71
  248.0 2.4 fusion.72
  250.4 2.3 fusion.70
  252.7 0.8 fusion.71
  253.5 2.4 fusion.72
  255.9 2.7 convolution_convert_fusion
  258.7 69.4 %all-gather.13.cloned.1.call-done = bf16[2048,3,256]{2,0,1:T(8,128)(2,1)} async-done(((bf16[32,3,256]{2,0,1:T(8,128)(2,1)}), bf16[2048,3,256]{2,0,1:T(8,128)(2,1)}) %all-gather.13.cloned.1.call-update) | async-done | bytes 3145744 | tf_op jit(solution)/shard_map/all_gather | solution.py:140
  328.0 4.7 %copy.77 = bf16[2048,3,256]{0,2,1:T(8,128)(2,1)} copy(bf16[2048,3,256]{2,0,1:T(8,128)(2,1)} %all-gather.13.cloned.1.call-done) | data formatting | bytes 6291456 | tf_op jit(solution)/shard_map/all_gather | solution.py:140
  332.7 90.1 %all-gather.15.cloned.1.call-done = bf16[2048,2048]{1,0:T(8,128)(2,1)} async-done(((bf16[256,2048]{1,0:T(8,128)(2,1)}), bf16[2048,2048]{1,0:T(8,128)(2,1)}) %all-gather.15.cloned.1.call-update) | async-done | bytes 8388624 | tf_op jit(solution)/shard_map/all_gather | solution.py:132
  422.8 5.2 %reduce_sum.69 = bf16[256,2048]{1,0:T(8,128)(2,1)S(1)} reduce(bf16[8,256,2048]{2,1,0:T(8,128)(2,1)} %bitcast.73, bf16[]{:T(256)} %constant.191.clone.1), dimensions={0}, to_apply=%region_11.12 | reduce | flops 3670016 | bytes 9437186 | tf_op jit(solution)/shard_map/reduce_sum | solution.py:132
  428.1 2.0 convert_reduce_fusion.1
  431.2 1.2 fusion.33
  432.5 0.9 copy.79
  433.4 1.6 constant_dynamic-slice_fusion
  (95 shorter events, 7.0 us)
Async XLA Ops:
  7.2 32.4 %copy-start = (bf16[48,2,32,256]{3,2,1,0:T(8,128)(2,1)S(1)}, bf16[48,2,32,256]{3,2,1,0:T(8,128)(2,1)}, u32[]{:S(2)}) copy-start(bf16[48,2,32,256]{3,2,1,0:T(8,128)(2,1)} %param.26) | copy-start | bytes 4718596
  7.2 50.4 %all-gather.7.cloned.1.call-start = ((), (), s32[]{:S(2)}) async-start(), calls=%async_computation.2 | async-start | bytes 1179648 | tf_op jit(solution)/shard_map/all_gather | solution.py:65
  7.9 150.9 %all-gather.9.cloned.1.call-start = ((), (), s32[]{:S(2)}) async-start(), calls=%async_computation.3 | async-start | bytes 3194880 | tf_op jit(solution)/shard_map/all_gather | solution.py:71
  42.4 7.4 %copy-start.9 = (f32[3,256]{1,0:T(4,128)S(1)}, f32[3,256]{1,0:T(4,128)}, u32[]{:S(2)}) copy-start(f32[3,256]{1,0:T(4,128)} %param.25) | copy-start | bytes 9220
  42.4 7.5 %copy-start.6 = (s32[256]{0:T(256)S(1)}, s32[256]{0:T(256)}, u32[]{:S(2)}) copy-start(s32[256]{0:T(256)} %param.33) | copy-start | bytes 3076
  42.4 10.7 %copy-start.7 = (s32[4]{0:T(128)S(1)}, s32[4]{0:T(128)}, u32[]{:S(2)}) copy-start(s32[4]{0:T(128)} %param.34) | copy-start | bytes 52
  42.4 11.5 %copy-start.11 = (pred[4096]{0:T(1024)(128)(4,1)S(1)}, pred[4096]{0:T(1024)(128)(4,1)}, u32[]{:S(2)}) copy-start(pred[4096]{0:T(1024)(128)(4,1)} %constant.224) | copy-start | bytes 12292
  42.4 11.5 %copy-start.12 = (pred[4096]{0:T(1024)(128)(4,1)S(1)}, pred[4096]{0:T(1024)(128)(4,1)}, u32[]{:S(2)}) copy-start(pred[4096]{0:T(1024)(128)(4,1)} %constant.225) | copy-start | bytes 12292
  42.4 11.5 %copy-start.13 = (pred[4096]{0:T(1024)(128)(4,1)S(1)}, pred[4096]{0:T(1024)(128)(4,1)}, u32[]{:S(2)}) copy-start(pred[4096]{0:T(1024)(128)(4,1)} %constant.226) | copy-start | bytes 12292
  42.4 127.0 %all-to-all-start.1 = ((bf16[64,2,2,32,256]{4,3,2,1,0:T(8,128)(2,1)}), bf16[64,2,2,32,256]{4,3,2,1,0:T(8,128)(2,1)}, u32[]{:S(2)}, u32[]{:S(2)}) async-start(bf16[64,2,2,32,256]{4,3,2,1,0:T(8,128)(2,1)} %bitcast.72), calls=%async_computation.1 | async-start | bytes 8388608 | tf_op jit(solution)/shard_map/all_to_all | solution.py:94
  48.3 207.6 %all-gather.11.cloned.1.call-start = ((), (), s32[]{:S(2)}) async-start(), calls=%async_computation.4 | async-start | bytes 1064960 | tf_op jit(solution)/shard_map/all_gather | solution.py:128
  49.0 279.0 %all-gather.13.cloned.1.call-start = ((), (), s32[]{:S(2)}) async-start(), calls=%async_computation.5 | async-start | bytes 3194880 | tf_op jit(solution)/shard_map/all_gather | solution.py:140
  49.6 373.3 %all-gather.15.cloned.1.call-start = ((), (), s32[]{:S(2)}) async-start(), calls=%async_computation.6 | async-start | bytes 9437184 | tf_op jit(solution)/shard_map/all_gather | solution.py:132
  60.7 102.9 %copy-start.2 = (bf16[256,2048]{1,0:T(8,128)(2,1)S(1)}, bf16[256,2048]{1,0:T(8,128)(2,1)}, u32[]{:S(2)}) copy-start(bf16[256,2048]{1,0:T(8,128)(2,1)} %all-gather.7.cloned.1.call-done) | copy-start | bytes 3145732
  60.7 102.9 %copy-start.14 = (f32[2048]{0:T(1024)S(1)}, f32[2048]{0:T(1024)}, u32[]{:S(2)}) copy-start(f32[2048]{0:T(1024)} %param.23) | copy-start | bytes 24580
  60.7 102.8 %copy-start.15 = (f32[2048]{0:T(1024)S(1)}, f32[2048]{0:T(1024)}, u32[]{:S(2)}) copy-start(f32[2048]{0:T(1024)} %param.22) | copy-start | bytes 24580
  231.2 2.7 copy-start.5
  255.8 2.8 copy-start.10
  422.8 5.2 %copy-start.8 = (f32[2048]{0:T(1024)S(1)}, f32[2048]{0:T(1024)}, u32[]{:S(2)}) copy-start(f32[2048]{0:T(1024)} %param.28) | copy-start | bytes 24580
  428.1 3.1 copy-start.4
  428.1 3.1 copy-start.16
  428.1 3.0 copy-start.17
  430.2 1.0 copy-start.3
  430.6 4.4 copy-start.1
Sparse Core Ops, SparseCore 0:
  10.0 43.6 all-gather.6
  57.1 101.6 all-gather.8
  162.2 80.7 all-gather.10
  246.2 81.8 all-gather.12
  329.9 92.8 all-gather.14
